TPU v7x, 512 devices: a whole 4x4x16 slice. The times are simulated.
512 devices in a mesh: pipe: 8 (over y, x_lo), expert: 64 (over x_hi, z, core).
Axes of the slice: x: 4 (x_hi: 2, x_lo: 2; x = x_hi * 2 + x_lo), y: 4, z: 16, core: 2. Of those that a mesh axis runs over, the one named last changes fastest.
Arguments:
- fwd_tokens: bfloat16 [8, 1024, 3584], P('pipe', 'expert'), may hold values from -6 to 6
- fwd_routes: int32 [8, 1024, 2], P('pipe', 'expert'), may hold values from 0 to 7, all different within a row; in each aligned block of 16 rows (0 to 15, 16 to 31, ..., all dimensions but the last counted through in order) at most 6 rows name the same one
- fwd_scores: float32 [8, 1024, 2], P('pipe', 'expert'), may hold values from 0.1 to 1
- bwd_tokens: bfloat16 [8, 1024, 3584], P('pipe', 'expert'), may hold values from -6 to 6
- bwd_routes: int32 [8, 1024, 2], P('pipe', 'expert'), may hold values from 0 to 7, all different within a row; in each aligned block of 16 rows (0 to 15, 16 to 31, ..., all dimensions but the last counted through in order) at most 6 rows name the same one
- bwd_scores: float32 [8, 1024, 2], P('pipe', 'expert'), may hold values from 0.1 to 1
- out_grad: bfloat16 [8, 1024, 3584], P('pipe', 'expert'), may hold values from -6 to 6
- gate_weight: bfloat16 [8, 3584, 8192], P('pipe', None, 'expert'), may hold values from -0.09375 to 0.09375
- up_weight: bfloat16 [8, 3584, 8192], P('pipe', None, 'expert'), may hold values from -0.09375 to 0.09375
- down_weight: bfloat16 [8, 8192, 3584], P('pipe', 'expert'), may hold values from -0.1875 to 0.1875
Outputs:
- next_input: bfloat16 [8, 1024, 3584], P('pipe', 'expert')
- prev_grad: bfloat16 [8, 1024, 3584], P('pipe', 'expert')
Inputs may be any that keep to these rules, and one draw needn't show every extreme that they name: `fwd_routes`: each row names 2 different experts. Among the 16 rows of one device in one section, no expert is named more than 6 times, a bound that some block reaches. `bwd_routes`: each row names 2 different experts. Among the 16 rows of one device in one section, no expert is named more than 6 times, a bound that some block reaches.
All inputs are finite; a program needn't handle non-finite values.
Results may differ from a plain program's by a relative error of at most 0.011.
Values may be sent and summed in bfloat16 or wider, within the bound.
No kernel may reach another device: no remote copies, remote signals or barrier semaphores. Data moves between devices by JAX's collectives and lax.ppermute only.
A program may use at most 128 MiB of HBM per device.

v0:
```python
import jax
import jax.numpy as jnp
from jax import lax
from jax.sharding import PartitionSpec as P

GROUP = 8


def from_behind(value, axis, steps):
    count = lax.axis_size(axis)
    pairs = [(source, (source + steps) % count) for source in range(count)]
    return lax.ppermute(value, axis, pairs)


def route_tables(routes, scores, capacity, experts):
    tokens, topk = routes.shape
    flat = routes.reshape(-1)
    onehot = (flat[:, None] == jnp.arange(experts, dtype=jnp.int32)[None, :]).astype(jnp.int32)
    rank = jnp.cumsum(onehot, axis=0) - onehot
    within = jnp.sum(rank * onehot, axis=1)
    slot_ids = (flat * capacity + within).reshape(tokens, topk)
    places = jnp.arange(experts * capacity, dtype=jnp.int32)
    hits = (slot_ids[:, :, None] == places[None, None, :]).astype(jnp.float32)
    normed = scores / jnp.sum(scores, axis=1, keepdims=True)
    member = jnp.sum(hits, axis=1)
    weighted = jnp.sum(hits * normed[:, :, None], axis=1)
    return (member, weighted)


def pick_rows(member, rows):
    slots = jnp.einsum(
        "te,td->ed", member.astype(jnp.bfloat16), rows, preferred_element_type=jnp.float32
    )
    return slots.astype(jnp.bfloat16)


def expert_forward(rows3, w_gate, w_up, w_down):
    width = rows3.shape[-1]
    flat = rows3.reshape(-1, width)
    first = jnp.dot(flat, w_gate, preferred_element_type=jnp.float32)
    second = jnp.dot(flat, w_up, preferred_element_type=jnp.float32)
    hidden = (jax.nn.silu(first) * second).astype(jnp.bfloat16)
    parts = jnp.dot(hidden, w_down, preferred_element_type=jnp.float32).astype(jnp.bfloat16)
    return parts.reshape(rows3.shape)


def expert_backward(rows3, grads3, w_gate, w_up, w_down):
    width = rows3.shape[-1]
    flat = rows3.reshape(-1, width)
    first = jnp.dot(flat, w_gate, preferred_element_type=jnp.float32)
    second = jnp.dot(flat, w_up, preferred_element_type=jnp.float32)
    d_hidden = lax.dot_general(
        grads3.reshape(-1, width),
        w_down,
        (((1,), (1,)), ((), ())),
        preferred_element_type=jnp.float32,
    )
    sigm = 1.0 / (1.0 + jnp.exp(-first))
    d_first = (d_hidden * second * sigm * (1.0 + first * (1.0 - sigm))).astype(jnp.bfloat16)
    d_second = (d_hidden * first * sigm).astype(jnp.bfloat16)
    back = lax.dot_general(
        d_first, w_gate, (((1,), (1,)), ((), ())), preferred_element_type=jnp.float32
    )
    back = back + lax.dot_general(
        d_second, w_up, (((1,), (1,)), ((), ())), preferred_element_type=jnp.float32
    )
    return back.astype(jnp.bfloat16).reshape(rows3.shape)


def expert_work(arrived, weights):
    w_gate, w_up, w_down = weights
    kinds = arrived.shape[0]
    if kinds == 1:
        return expert_forward(arrived[0], w_gate, w_up, w_down)[None]
    return expert_backward(arrived[0], arrived[1], w_gate, w_up, w_down)[None]


def pass_rows(payload, weights):
    kinds, experts, capacity, width = payload.shape
    spread = jnp.broadcast_to(payload[:, :, None], (kinds, experts, GROUP, capacity, width))
    spread = spread.reshape(kinds, experts * GROUP, capacity, width)
    returned = lax.all_to_all(
        expert_work(
            lax.all_to_all(spread, "expert", split_axis=1, concat_axis=1, tiled=True), weights
        ),
        "expert",
        split_axis=1,
        concat_axis=1,
        tiled=True,
    )
    outkinds = returned.shape[0]
    summed = jnp.sum(
        returned.reshape(outkinds, experts, GROUP, capacity, width).astype(jnp.float32), axis=2
    )
    return summed.reshape(outkinds, experts * capacity, width)


def body(
    fwd_tokens,
    fwd_routes,
    fwd_scores,
    bwd_tokens,
    bwd_routes,
    bwd_scores,
    out_grad,
    gate_weight,
    up_weight,
    down_weight,
):
    experts = lax.axis_size("expert") // GROUP
    tokens = fwd_tokens.shape[1]
    topk = fwd_routes.shape[2]
    width = fwd_tokens.shape[2]
    capacity = min(tokens, max(6, (tokens * topk + experts - 1) // experts + 2))
    weights = (gate_weight[0], up_weight[0], down_weight[0])
    member_f, weight_f = route_tables(fwd_routes[0], fwd_scores[0], capacity, experts)
    member_b, weight_b = route_tables(bwd_routes[0], bwd_scores[0], capacity, experts)
    send_f = pick_rows(member_f, fwd_tokens[0]).reshape(experts, capacity, width)
    send_x = pick_rows(member_b, bwd_tokens[0]).reshape(experts, capacity, width)
    route_grad = jnp.einsum(
        "te,td->ed", weight_b, out_grad[0].astype(jnp.float32), precision=lax.Precision.HIGHEST
    )
    send_g = route_grad.astype(jnp.bfloat16).reshape(experts, capacity, width)
    sum_f = pass_rows(send_f[None], weights)[0]
    sum_b = pass_rows(jnp.stack((send_x, send_g)), weights)[0]
    layer_out = jnp.dot(weight_f, sum_f, precision=lax.Precision.HIGHEST).astype(jnp.bfloat16)[None]
    input_grad = jnp.dot(member_b, sum_b, precision=lax.Precision.HIGHEST).astype(jnp.bfloat16)[
        None
    ]
    next_input = from_behind(layer_out, "pipe", 1)
    prev_grad = from_behind(input_grad, "pipe", -1)
    return (next_input, prev_grad)


def solution(mesh):
    placed = (
        P("pipe", "expert", None),
        P("pipe", "expert", None),
        P("pipe", "expert", None),
        P("pipe", "expert", None),
        P("pipe", "expert", None),
        P("pipe", "expert", None),
        P("pipe", "expert", None),
        P("pipe", None, "expert"),
        P("pipe", None, "expert"),
        P("pipe", "expert", None),
    )
    return jax.shard_map(
        body,
        mesh=mesh,
        in_specs=placed,
        out_specs=(P("pipe", "expert", None), P("pipe", "expert", None)),
        check_vma=False,
    )
```

profile of v0, /device:TPU:30, one launch (start us, length us, event | category | flops | bytes accessed | tf_op | source)
XLA Modules:
  0.0 810.3 jit_solution(13249150855847399699)
XLA Ops:
  7.6 19.0 %all-to-all-start = ((bf16[1,64,6,3584]{3,2,0,1:T(8,128)(2,1)}), bf16[1,64,6,3584]{3,2,0,1:T(8,128)(2,1)}, u32[]{:S(2)}, u32[]{:S(2)}) async-start(bf16[1,64,6,3584]{3,2,0,1:T(8,128)(2,1)} %bitcast.66), calls=%async_computation | async-start | bytes 7340032 | tf_op jit(solution)/shard_map/all_to_all | solution.py:84
  29.4 161.7 %all-to-all-done = bf16[1,64,6,3584]{3,2,0,1:T(8,128)(2,1)} async-done(((bf16[1,64,6,3584]{3,2,0,1:T(8,128)(2,1)}), bf16[1,64,6,3584]{3,2,0,1:T(8,128)(2,1)}, u32[]{:S(2)}, u32[]{:S(2)}) %all-to-all-start) | async-done | bytes 2752544 | tf_op jit(solution)/shard_map/all_to_all | solution.py:84
  191.1 5.2 broadcast_in_dim.16
  196.3 9.4 %all-to-all-start.2 = ((bf16[2,64,6,3584]{3,0,2,1:T(2,128)(2,1)}), bf16[2,64,6,3584]{3,0,2,1:T(2,128)(2,1)}, u32[]{:S(2)}, u32[]{:S(2)}) async-start(bf16[2,64,6,3584]{3,0,2,1:T(2,128)(2,1)} %bitcast.63), calls=%async_computation.2 | async-start | bytes 11010048 | tf_op jit(solution)/shard_map/all_to_all | solution.py:84
  205.8 5.6 reshape_squeeze.11
  211.3 2.7 fusion.19
  214.1 6.3 convolution_convert_fusion
  220.4 5.4 broadcast_in_dim_reshape.8
  225.8 224.4 %all-to-all-done.2 = bf16[2,64,6,3584]{3,0,2,1:T(2,128)(2,1)} async-done(((bf16[2,64,6,3584]{3,0,2,1:T(2,128)(2,1)}), bf16[2,64,6,3584]{3,0,2,1:T(2,128)(2,1)}, u32[]{:S(2)}, u32[]{:S(2)}) %all-to-all-start.2) | async-done | bytes 5505056 | tf_op jit(solution)/shard_map/all_to_all | solution.py:84
  450.2 8.1 all-to-all-start.1
  458.4 37.1 %slice_reduce_fusion = (bf16[64,6,3584]{2,1,0:T(8,128)(2,1)}, bf16[64,6,3584]{2,1,0:T(8,128)(2,1)}) fusion(bf16[2,64,6,3584]{3,0,2,1:T(2,128)(2,1)} %all-to-all-done.2), kind=kLoop, calls=%fused_computation.5 | loop fusion | bytes 11010048 | tf_op jit(solution)/shard_map/slice | solution.py:75
  495.4 5.5 reshape_squeeze.13
  500.9 5.4 reshape_squeeze.12
  506.4 2.8 fusion.17
  510.1 7.3 fusion.7
  517.3 5.0 fusion
  522.3 5.5 broadcast_in_dim_reshape.9
  527.8 95.1 %all-to-all-done.1 = bf16[1,64,6,3584]{3,2,0,1:T(8,128)(2,1)} async-done(((bf16[1,64,6,3584]{3,2,0,1:T(8,128)(2,1)}), bf16[1,64,6,3584]{3,2,0,1:T(8,128)(2,1)}, u32[]{:S(2)}, u32[]{:S(2)}) %all-to-all-start.1) | async-done | bytes 2752544 | tf_op jit(solution)/shard_map/all_to_all | solution.py:82
  622.8 9.4 %all-to-all-start.3 = ((bf16[1,64,6,3584]{3,2,0,1:T(8,128)(2,1)}), bf16[1,64,6,3584]{3,2,0,1:T(8,128)(2,1)}, u32[]{:S(2)}, u32[]{:S(2)}) async-start(bf16[1,64,6,3584]{3,2,0,1:T(8,128)(2,1)} %bitcast.65), calls=%async_computation.3 | async-start | bytes 7340032 | tf_op jit(solution)/shard_map/all_to_all | solution.py:82
  632.3 2.9 convert_reduce_fusion.1
  638.1 158.7 %all-to-all-done.3 = bf16[1,64,6,3584]{3,2,0,1:T(8,128)(2,1)} async-done(((bf16[1,64,6,3584]{3,2,0,1:T(8,128)(2,1)}), bf16[1,64,6,3584]{3,2,0,1:T(8,128)(2,1)}, u32[]{:S(2)}, u32[]{:S(2)}) %all-to-all-start.3) | async-done | bytes 2752544 | tf_op jit(solution)/shard_map/all_to_all | solution.py:82
  796.8 2.9 convert_reduce_fusion
  800.2 2.7 collective-permute-start.1
  803.0 6.0 collective-permute-done.1
  (56 shorter events, 15.3 us)
Async XLA Ops:
  0.6 213.5 %copy-start = (bf16[1,3584,128]{2,1,0:T(8,128)(2,1)S(1)}, bf16[1,3584,128]{2,1,0:T(8,128)(2,1)}, u32[]{:S(2)}) copy-start(bf16[1,3584,128]{2,1,0:T(8,128)(2,1)} %param.18) | copy-start | bytes 2752516
  7.6 19.0 %copy-start.6 = (s32[1,16,2]{1,2,0:T(2,128)S(1)}, s32[1,16,2]{1,2,0:T(2,128)}, u32[]{:S(2)}) copy-start(s32[1,16,2]{1,2,0:T(2,128)} %param.14) | copy-start | bytes 388
  7.6 19.7 %copy-start.7 = (f32[1,16,2]{1,2,0:T(2,128)S(1)}, f32[1,16,2]{1,2,0:T(2,128)}, u32[]{:S(2)}) copy-start(f32[1,16,2]{1,2,0:T(2,128)} %param.15) | copy-start | bytes 388
  7.6 19.8 %copy-start.4 = (bf16[1,16,3584]{2,1,0:T(8,128)(2,1)S(1)}, bf16[1,16,3584]{2,1,0:T(8,128)(2,1)}, u32[]{:S(2)}) copy-start(bf16[1,16,3584]{2,1,0:T(8,128)(2,1)} %param.13) | copy-start | bytes 344068
  7.6 20.3 %copy-start.5 = (bf16[1,16,3584]{2,1,0:T(8,128)(2,1)S(1)}, bf16[1,16,3584]{2,1,0:T(8,128)(2,1)}, u32[]{:S(2)}) copy-start(bf16[1,16,3584]{2,1,0:T(8,128)(2,1)} %param.16) | copy-start | bytes 344068
  7.6 183.5 %all-to-all-start = ((bf16[1,64,6,3584]{3,2,0,1:T(8,128)(2,1)}), bf16[1,64,6,3584]{3,2,0,1:T(8,128)(2,1)}, u32[]{:S(2)}, u32[]{:S(2)}) async-start(bf16[1,64,6,3584]{3,2,0,1:T(8,128)(2,1)} %bitcast.66), calls=%async_computation | async-start | bytes 7340032 | tf_op jit(solution)/shard_map/all_to_all | solution.py:84
  196.3 253.9 %all-to-all-start.2 = ((bf16[2,64,6,3584]{3,0,2,1:T(2,128)(2,1)}), bf16[2,64,6,3584]{3,0,2,1:T(2,128)(2,1)}, u32[]{:S(2)}, u32[]{:S(2)}) async-start(bf16[2,64,6,3584]{3,0,2,1:T(2,128)(2,1)} %bitcast.63), calls=%async_computation.2 | async-start | bytes 11010048 | tf_op jit(solution)/shard_map/all_to_all | solution.py:84
  205.8 5.6 copy-start.2
  211.3 2.7 copy-start.3
  450.2 172.6 %all-to-all-start.1 = ((bf16[1,64,6,3584]{3,2,0,1:T(8,128)(2,1)}), bf16[1,64,6,3584]{3,2,0,1:T(8,128)(2,1)}, u32[]{:S(2)}, u32[]{:S(2)}) async-start(bf16[1,64,6,3584]{3,2,0,1:T(8,128)(2,1)} %bitcast.64), calls=%async_computation.1 | async-start | bytes 7340032 | tf_op jit(solution)/shard_map/all_to_all | solution.py:82
  506.4 2.8 copy-start.1
  622.8 173.9 %all-to-all-start.3 = ((bf16[1,64,6,3584]{3,2,0,1:T(8,128)(2,1)}), bf16[1,64,6,3584]{3,2,0,1:T(8,128)(2,1)}, u32[]{:S(2)}, u32[]{:S(2)}) async-start(bf16[1,64,6,3584]{3,2,0,1:T(8,128)(2,1)} %bitcast.65), calls=%async_computation.3 | async-start | bytes 7340032 | tf_op jit(solution)/shard_map/all_to_all | solution.py:82
  635.7 167.2 %collective-permute-start = (bf16[1,16,3584]{2,1,0:T(8,128)(2,1)S(1)}, bf16[1,16,3584]{2,1,0:T(8,128)(2,1)S(1)}, u32[]{:S(2)}, u32[]{:S(2)}) collective-permute-start(bf16[1,16,3584]{2,1,0:T(8,128)(2,1)S(1)} %fusion.1), channel_id=1, source_target_pairs={{0,64},{64,128},{128,192},{192,256},{256,320},{320,384},{384,448},... | collective-permute-start | bytes 344072 | tf_op jit(solution)/shard_map/ppermute | solution.py:12
  800.2 8.8 %collective-permute-start.1 = (bf16[1,16,3584]{2,1,0:T(8,128)(2,1)S(1)}, bf16[1,16,3584]{2,1,0:T(8,128)(2,1)S(1)}, u32[]{:S(2)}, u32[]{:S(2)}) collective-permute-start(bf16[1,16,3584]{2,1,0:T(8,128)(2,1)S(1)} %fusion.2), channel_id=1, source_target_pairs={{0,448},{64,0},{128,64},{192,128},{256,192},{320,256},{384,320},{4... | collective-permute-start | bytes 344072 | tf_op jit(solution)/shard_map/ppermute | solution.py:12
where the time goes:
time: 812 us; the launch traced here: 810 us
  waiting for transfers between devices  646 us (80%)
  local copies, waits for them, and re-layouts  75.8 us (9%)
  starting transfers between devices  51.2 us (6%)
  matrix products  27.7 us (3%)
  other arithmetic  8.81 us (1%)
    all_to_all x2, waiting for transfers between devices, pass_rows(): lax.all_to_all(spread, 'expert', split_axis=1, concat_axis=1, tiled=True)  386 us
    all_to_all x2, waiting for transfers between devices, pass_rows(): lax.all_to_all(expert_work(lax.all_to_all(spread, 'expert', split_axis=1,...  254 us
    slice x1, local copies, waits for them, and re-layouts, expert_work(): return expert_backward(arrived[0], arrived[1], w_gate, w_up, w_down)[None]  37.1 us
    all_to_all x2, starting transfers between devices, pass_rows(): lax.all_to_all(spread, 'expert', split_axis=1, concat_axis=1, tiled=True)  28.5 us
    all_to_all x2, starting transfers between devices, pass_rows(): lax.all_to_all(expert_work(lax.all_to_all(spread, 'expert', split_axis=1,...  17.5 us
  transfers between devices with their start and end apart: 6, of which 5 were waited for; matrix products, arithmetic and copies ran while one was open for 12% of the time, Pallas kernels for 0%

commit v1 on v0

--- a/solution.py
+++ b/solution.py
@@ -79,14 +79,23 @@
     kinds, experts, capacity, width = payload.shape
     spread = jnp.broadcast_to(payload[:, :, None], (kinds, experts, GROUP, capacity, width))
     spread = spread.reshape(kinds, experts * GROUP, capacity, width)
-    returned = lax.all_to_all(
-        expert_work(
-            lax.all_to_all(spread, "expert", split_axis=1, concat_axis=1, tiled=True), weights
+    returned = jnp.concatenate(
+        lax.all_to_all(
+            jnp.stack(
+                jnp.split(
+                    expert_work(
+                        lax.all_to_all(spread, "expert", split_axis=1, concat_axis=1, tiled=True),
+                        weights,
+                    ),
+                    lax.axis_size("expert"),
+                    axis=1,
+                )
+            ),
+            "expert",
+            0,
+            0,
         ),
-        "expert",
-        split_axis=1,
-        concat_axis=1,
-        tiled=True,
+        axis=1,
     )
     outkinds = returned.shape[0]
     summed = jnp.sum(

time: 812 us -> 823 us (1.014)
  waiting for transfers between devices: 646 us -> 460 us
  local copies, waits for them, and re-layouts: 75.8 us -> 260 us
    unnamed x20 -> x144, local copies, waits for them, and re-layouts: 2.25 us -> 184 us
    all_to_all x2, waiting for transfers between devices: 254 us -> 160 us  [pass_rows(): lax.all_to_all(jnp.stack(jnp.split(expert_work(lax.all_to_all(spread, 'ex...]
    all_to_all x2, waiting for transfers between devices: 386 us -> 294 us  [pass_rows(): lax.all_to_all(spread, 'expert', split_axis=1, concat_axis=1, tiled=True)]
  transfers between devices with their start and end apart: 6 -> 6, of which waited for: 5 -> 5; matrix products, arithmetic and copies ran while one was open for 12% -> 35% of each run, Pallas kernels for 0% -> 0%
where the time goes in v1:
time: 823 us; the launch traced here: 815 us
  waiting for transfers between devices  460 us (56%)
  local copies, waits for them, and re-layouts  260 us (32%)
  starting transfers between devices  56.1 us (7%)
  matrix products  29.4 us (4%)
  other arithmetic  8.81 us (1%)
    all_to_all x2, waiting for transfers between devices, pass_rows(): lax.all_to_all(spread, 'expert', split_axis=1, concat_axis=1, tiled=True)  294 us
    unnamed x144, local copies, waits for them, and re-layouts  184 us
    all_to_all x2, waiting for transfers between devices, pass_rows(): lax.all_to_all(jnp.stack(jnp.split(expert_work(lax.all_to_all(spread, 'ex...  160 us
    slice x1, local copies, waits for them, and re-layouts, expert_work(): return expert_backward(arrived[0], arrived[1], w_gate, w_up, w_down)[None]  37.1 us
    all_to_all x2, starting transfers between devices, pass_rows(): lax.all_to_all(spread, 'expert', split_axis=1, concat_axis=1, tiled=True)  28.5 us
    all_to_all x2, starting transfers between devices, pass_rows(): lax.all_to_all(jnp.stack(jnp.split(expert_work(lax.all_to_all(spread, 'ex...  22.5 us
  transfers between devices with their start and end apart: 6, of which 5 were waited for; matrix products, arithmetic and copies ran while one was open for 35% of the time, Pallas kernels for 0%

profile of v1, /device:TPU:30, one launch (start us, length us, event | category | flops | bytes accessed | tf_op | source)
XLA Modules:
  0.0 815.2 jit_solution(1730408528768611244)
XLA Ops:
  7.6 19.0 %all-to-all-start = ((bf16[1,64,6,3584]{3,2,0,1:T(8,128)(2,1)}), bf16[1,64,6,3584]{3,2,0,1:T(8,128)(2,1)}, u32[]{:S(2)}, u32[]{:S(2)}) async-start(bf16[1,64,6,3584]{3,2,0,1:T(8,128)(2,1)} %bitcast.574), calls=%async_computation | async-start | bytes 7340032 | tf_op jit(solution)/shard_map/all_to_all | solution.py:87
  29.4 161.7 %all-to-all-done = bf16[1,64,6,3584]{3,2,0,1:T(8,128)(2,1)} async-done(((bf16[1,64,6,3584]{3,2,0,1:T(8,128)(2,1)}), bf16[1,64,6,3584]{3,2,0,1:T(8,128)(2,1)}, u32[]{:S(2)}, u32[]{:S(2)}) %all-to-all-start) | async-done | bytes 2752544 | tf_op jit(solution)/shard_map/all_to_all | solution.py:87
  191.1 5.2 broadcast_in_dim.16
  196.3 9.4 %all-to-all-start.2 = ((bf16[2,64,6,3584]{3,0,2,1:T(2,128)(2,1)}), bf16[2,64,6,3584]{3,0,2,1:T(2,128)(2,1)}, u32[]{:S(2)}, u32[]{:S(2)}) async-start(bf16[2,64,6,3584]{3,0,2,1:T(2,128)(2,1)} %bitcast.573), calls=%async_computation.2 | async-start | bytes 11010048 | tf_op jit(solution)/shard_map/all_to_all | solution.py:87
  205.8 5.6 reshape_squeeze.11
  211.3 2.7 fusion.19
  214.1 6.4 convolution_convert_fusion
  220.5 5.4 broadcast_in_dim_reshape.8
  318.2 132.0 %all-to-all-done.2 = bf16[2,64,6,3584]{3,0,2,1:T(2,128)(2,1)} async-done(((bf16[2,64,6,3584]{3,0,2,1:T(2,128)(2,1)}), bf16[2,64,6,3584]{3,0,2,1:T(2,128)(2,1)}, u32[]{:S(2)}, u32[]{:S(2)}) %all-to-all-start.2) | async-done | bytes 5505056 | tf_op jit(solution)/shard_map/all_to_all | solution.py:87
  450.2 8.3 %all-to-all-start.1 = ((bf16[64,1,1,6,3584]{4,3,2,1,0:T(8,128)(2,1)}), bf16[64,1,1,6,3584]{4,3,2,1,0:T(8,128)(2,1)}, u32[]{:S(2)}, u32[]{:S(2)}) async-start(bf16[64,1,1,6,3584]{4,3,2,1,0:T(8,128)(2,1)} %constant_dynamic-update-slice_fusion), calls=%async_computation.1 | async-start | bytes 7340032 | tf_op jit(solution)/shard_map/all_to_all | solution.py:83
  458.5 37.1 %slice_reduce_fusion = (bf16[64,6,3584]{2,1,0:T(8,128)(2,1)}, bf16[64,6,3584]{2,1,0:T(8,128)(2,1)}) fusion(bf16[2,64,6,3584]{3,0,2,1:T(2,128)(2,1)} %all-to-all-done.2), kind=kLoop, calls=%fused_computation.5 | loop fusion | bytes 11010048 | tf_op jit(solution)/shard_map/slice | solution.py:75
  495.6 5.5 reshape_squeeze.13
  501.1 2.6 fusion.17
  503.8 5.5 reshape_squeeze.12
  509.2 2.6 fusion.8
  511.9 7.3 fusion.7
  519.1 5.0 fusion
  524.1 5.4 broadcast_in_dim_reshape.9
  623.0 14.2 %all-to-all-start.3 = ((bf16[64,1,1,6,3584]{4,3,2,1,0:T(8,128)(2,1)}), bf16[64,1,1,6,3584]{4,3,2,1,0:T(8,128)(2,1)}, u32[]{:S(2)}, u32[]{:S(2)}) async-start(bf16[64,1,1,6,3584]{4,3,2,1,0:T(8,128)(2,1)} %constant_dynamic-update-slice_fusion.64), calls=%async_computation.3 | async-start | bytes 7340032 | tf_op jit(solution)/shard_map/all_to_all | solution.py:83
  637.2 2.9 convert_reduce_fusion.1
  643.1 158.6 %all-to-all-done.3 = bf16[64,1,1,6,3584]{4,3,2,1,0:T(8,128)(2,1)} async-done(((bf16[64,1,1,6,3584]{4,3,2,1,0:T(8,128)(2,1)}), bf16[64,1,1,6,3584]{4,3,2,1,0:T(8,128)(2,1)}, u32[]{:S(2)}, u32[]{:S(2)}) %all-to-all-start.3) | async-done | bytes 2752544 | tf_op jit(solution)/shard_map/all_to_all | solution.py:83
  801.7 2.9 convert_reduce_fusion
  805.1 2.7 collective-permute-start.1
  807.9 6.0 collective-permute-done.1
  (182 shorter events, 200.1 us)
Async XLA Ops:
  0.6 213.5 %copy-start = (bf16[1,3584,128]{2,1,0:T(8,128)(2,1)S(1)}, bf16[1,3584,128]{2,1,0:T(8,128)(2,1)}, u32[]{:S(2)}) copy-start(bf16[1,3584,128]{2,1,0:T(8,128)(2,1)} %param.18) | copy-start | bytes 2752516
  7.6 19.0 %copy-start.5 = (s32[1,16,2]{1,2,0:T(2,128)S(1)}, s32[1,16,2]{1,2,0:T(2,128)}, u32[]{:S(2)}) copy-start(s32[1,16,2]{1,2,0:T(2,128)} %param.14) | copy-start | bytes 388
  7.6 19.7 %copy-start.6 = (f32[1,16,2]{1,2,0:T(2,128)S(1)}, f32[1,16,2]{1,2,0:T(2,128)}, u32[]{:S(2)}) copy-start(f32[1,16,2]{1,2,0:T(2,128)} %param.15) | copy-start | bytes 388
  7.6 19.8 %copy-start.3 = (bf16[1,16,3584]{2,1,0:T(8,128)(2,1)S(1)}, bf16[1,16,3584]{2,1,0:T(8,128)(2,1)}, u32[]{:S(2)}) copy-start(bf16[1,16,3584]{2,1,0:T(8,128)(2,1)} %param.13) | copy-start | bytes 344068
  7.6 20.3 %copy-start.4 = (bf16[1,16,3584]{2,1,0:T(8,128)(2,1)S(1)}, bf16[1,16,3584]{2,1,0:T(8,128)(2,1)}, u32[]{:S(2)}) copy-start(bf16[1,16,3584]{2,1,0:T(8,128)(2,1)} %param.16) | copy-start | bytes 344068
  7.6 183.5 %all-to-all-start = ((bf16[1,64,6,3584]{3,2,0,1:T(8,128)(2,1)}), bf16[1,64,6,3584]{3,2,0,1:T(8,128)(2,1)}, u32[]{:S(2)}, u32[]{:S(2)}) async-start(bf16[1,64,6,3584]{3,2,0,1:T(8,128)(2,1)} %bitcast.574), calls=%async_computation | async-start | bytes 7340032 | tf_op jit(solution)/shard_map/all_to_all | solution.py:87
  196.3 253.9 %all-to-all-start.2 = ((bf16[2,64,6,3584]{3,0,2,1:T(2,128)(2,1)}), bf16[2,64,6,3584]{3,0,2,1:T(2,128)(2,1)}, u32[]{:S(2)}, u32[]{:S(2)}) async-start(bf16[2,64,6,3584]{3,0,2,1:T(2,128)(2,1)} %bitcast.573), calls=%async_computation.2 | async-start | bytes 11010048 | tf_op jit(solution)/shard_map/all_to_all | solution.py:87
  205.8 5.6 copy-start.1
  211.3 2.7 copy-start.2
  450.2 172.8 %all-to-all-start.1 = ((bf16[64,1,1,6,3584]{4,3,2,1,0:T(8,128)(2,1)}), bf16[64,1,1,6,3584]{4,3,2,1,0:T(8,128)(2,1)}, u32[]{:S(2)}, u32[]{:S(2)}) async-start(bf16[64,1,1,6,3584]{4,3,2,1,0:T(8,128)(2,1)} %constant_dynamic-update-slice_fusion), calls=%async_computation.1 | async-start | bytes 7340032 | tf_op jit(solution)/shard_map/all_to_all | solution.py:83
  623.0 178.7 %all-to-all-start.3 = ((bf16[64,1,1,6,3584]{4,3,2,1,0:T(8,128)(2,1)}), bf16[64,1,1,6,3584]{4,3,2,1,0:T(8,128)(2,1)}, u32[]{:S(2)}, u32[]{:S(2)}) async-start(bf16[64,1,1,6,3584]{4,3,2,1,0:T(8,128)(2,1)} %constant_dynamic-update-slice_fusion.64), calls=%async_computation.3 | async-start | bytes 7340032 | tf_op jit(solution)/shard_map/all_to_all | solution.py:83
  640.6 167.2 %collective-permute-start = (bf16[1,16,3584]{2,1,0:T(8,128)(2,1)S(1)}, bf16[1,16,3584]{2,1,0:T(8,128)(2,1)S(1)}, u32[]{:S(2)}, u32[]{:S(2)}) collective-permute-start(bf16[1,16,3584]{2,1,0:T(8,128)(2,1)S(1)} %fusion.1), channel_id=1, source_target_pairs={{0,64},{64,128},{128,192},{192,256},{256,320},{320,384},{384,448},... | collective-permute-start | bytes 344072 | tf_op jit(solution)/shard_map/ppermute | solution.py:12
  805.1 8.8 %collective-permute-start.1 = (bf16[1,16,3584]{2,1,0:T(8,128)(2,1)S(1)}, bf16[1,16,3584]{2,1,0:T(8,128)(2,1)S(1)}, u32[]{:S(2)}, u32[]{:S(2)}) collective-permute-start(bf16[1,16,3584]{2,1,0:T(8,128)(2,1)S(1)} %fusion.2), channel_id=1, source_target_pairs={{0,448},{64,0},{128,64},{192,128},{256,192},{320,256},{384,320},{4... | collective-permute-start | bytes 344072 | tf_op jit(solution)/shard_map/ppermute | solution.py:12
